TPU v7x, 256 devices: a whole 4x4x8 slice. The times are simulated.
256 devices in a mesh: req: 32 (over y, x, core), tp: 8 (over z).
Axes of the slice: x: 4, y: 4, z: 8, core: 2. Of those that a mesh axis runs over, the one named last changes fastest.
Arguments:
- queries: bfloat16 [2048, 4096], P('req', 'tp'), may hold values from -8 to 8
- suffix_kv: bfloat16 [2048, 2, 1024], P('req', None, 'tp'), may hold values from -6 to 6
- prefix_cache: bfloat16 [32, 2048, 2, 1024], P('req', None, None, 'tp'), may hold values from -8 to 8
- prefix_owner: int32 [4], replicated, may hold values from 0 to 31, as said below
- request_prefix: int32 [64], P('req'), may hold values from 0 to 3
- suffix_len: int32 [64], P('req'), may hold values from 1 to 32, 1728 in all
- residual: bfloat16 [2048, 4096], P('req'), may hold values from -40 to 40
- norm_gain: float32 [4096], replicated, may hold values from 0.1 to 1.9
- router: float32 [4096, 8], replicated, may hold values from -0.09375 to 0.09375
- routes: int32 [2048, 2], P('req'), may hold values from 0 to 7, all different within a row; in each aligned block of 64 rows (0 to 63, 64 to 127, ...) at most 18 rows name the same one
- w_gate: bfloat16 [32, 4096, 2048], P('req', None, 'tp'), may hold values from -0.09375 to 0.09375
- w_up: bfloat16 [32, 4096, 2048], P('req', None, 'tp'), may hold values from -0.09375 to 0.09375
- w_down: bfloat16 [32, 2048, 4096], P('req', 'tp'), may hold values from -0.0625 to 0.0625
- w_out: bfloat16 [4096, 4096], P('tp'), may hold values from -1 to 1
Outputs:
- layer_out: bfloat16 [2048, 4096], P('req', 'tp')
Inputs may be any that keep to these rules, and one draw needn't show every extreme that they name: `prefix_owner`: the 4 owners are distinct. Among the 64 token slots of one req index, no expert is named by more than 18 routes, and in some req indices one expert is named by exactly 18; the two experts of a token differ.
All inputs are finite; a program needn't handle non-finite values. No bound on the sum of `suffix_len` on one device may be relied on, other than what follows from the above.
Results may differ from a plain program's by a relative error of at most 0.017.
Values may be sent and summed in bfloat16 or wider, within the bound.
No kernel may reach another device: no remote copies, remote signals or barrier semaphores. Data moves between devices by JAX's collectives and lax.ppermute only.
A program may use at most 128 MiB of HBM per device.

v0:
```python
import math
import jax
import jax.numpy as jnp
from jax import lax
from jax.sharding import PartitionSpec as P

HEADS = 32
KVH = 8
HD = 128
EXPERTS = 8
NPFX = 4
CAP = 18


def broadcast(x, axis, root):
    mine = lax.axis_index(axis) == root
    return lax.psum(jnp.where(mine, x, jnp.zeros_like(x)), axis)


def attend_local(queries, suffix_kv, chosen, suffix_len, requests, slot_len):
    kv_local = suffix_kv.shape[2] // HD
    group_size = HEADS // KVH
    plen_local = chosen.shape[1]
    query_block = queries.reshape(requests, slot_len, kv_local, group_size, HD)
    cache_block = chosen.reshape(requests, plen_local, 2, kv_local, HD)
    suffix_block = suffix_kv.reshape(requests, slot_len, 2, kv_local, HD)
    score_scale = 1.0 / math.sqrt(HD)
    prefix_score = (
        jnp.einsum(
            "rikgd,rjkd->rkgij",
            query_block,
            cache_block[:, :, 0],
            preferred_element_type=jnp.float32,
        )
        * score_scale
    )
    suffix_score = (
        jnp.einsum(
            "rikgd,rjkd->rkgij",
            query_block,
            suffix_block[:, :, 0],
            preferred_element_type=jnp.float32,
        )
        * score_scale
    )
    positions = jnp.arange(slot_len, dtype=jnp.int32)
    allowed = (positions[None, None, :] <= positions[None, :, None]) & (
        positions[None, None, :] < suffix_len[:, None, None]
    )
    suffix_score = jnp.where(allowed[:, None, None], suffix_score, -1e30)
    score_peak = jnp.maximum(prefix_score.max(-1), suffix_score.max(-1))[..., None]
    prefix_exp = jnp.exp(prefix_score - score_peak)
    suffix_exp = jnp.exp(suffix_score - score_peak)
    normaliser = prefix_exp.sum(-1, keepdims=True) + suffix_exp.sum(-1, keepdims=True)
    prefix_prob = (prefix_exp / normaliser).astype(jnp.bfloat16)
    suffix_prob = (suffix_exp / normaliser).astype(jnp.bfloat16)
    mixed_values = jnp.einsum(
        "rkgij,rjkd->rikgd", prefix_prob, cache_block[:, :, 1], preferred_element_type=jnp.float32
    )
    mixed_values = mixed_values + jnp.einsum(
        "rkgij,rjkd->rikgd", suffix_prob, suffix_block[:, :, 1], preferred_element_type=jnp.float32
    )
    return mixed_values.reshape(requests * slot_len, kv_local * group_size * HD).astype(
        jnp.bfloat16
    )


def routing_tables(routes, live_rows, route_weight):
    expert_ids = jnp.arange(EXPERTS, dtype=jnp.int32)
    member = (routes[:, :, None] == expert_ids) & live_rows[:, None, None]
    member_int = member.astype(jnp.int32)
    flat_member = member_int.reshape(-1, EXPERTS)
    earlier = jnp.cumsum(flat_member, axis=0) - flat_member
    slot_index = jnp.sum(earlier * flat_member, axis=1).reshape(routes.shape)
    slot_hit = (slot_index[:, :, None] == jnp.arange(CAP, dtype=jnp.int32)).astype(jnp.float32)
    member_float = member.astype(jnp.float32)
    placing = (
        jnp.einsum("tke,tkc->ect", member_float, slot_hit)
        .reshape(EXPERTS * CAP, routes.shape[0])
        .astype(jnp.bfloat16)
    )
    combining = jnp.einsum(
        "tke,tkc,tk->tec", member_float, slot_hit, route_weight, precision=lax.Precision.HIGHEST
    )
    return (placing, combining.reshape(routes.shape[0], EXPERTS * CAP))


def expert_apply(arrived, w_gate, w_up, w_down):
    flat_rows = arrived.reshape(-1, arrived.shape[2])
    gate_value = jnp.dot(flat_rows, w_gate[0], preferred_element_type=jnp.float32)
    up_value = jnp.dot(flat_rows, w_up[0], preferred_element_type=jnp.float32)
    hidden_units = (jax.nn.silu(gate_value) * up_value).astype(jnp.bfloat16)
    piece_out = jnp.dot(hidden_units, w_down[0], preferred_element_type=jnp.float32).astype(
        jnp.bfloat16
    )
    return piece_out.reshape(arrived.shape[0], arrived.shape[1], piece_out.shape[1])


def send_back(parts):
    return lax.all_to_all(parts, "req", split_axis=0, concat_axis=0, tiled=True)


def per_device(
    queries,
    suffix_kv,
    prefix_cache,
    prefix_owner,
    request_prefix,
    suffix_len,
    residual,
    norm_gain,
    router,
    routes,
    w_gate,
    w_up,
    w_down,
    w_out,
):
    tp_count = lax.axis_size("tp")
    tp_index = lax.axis_index("tp")
    req_count = lax.axis_size("req")
    model_width = residual.shape[1]
    share_width = model_width // tp_count
    share_start = tp_index * share_width
    requests = request_prefix.shape[0]
    slot_len = queries.shape[0] // requests
    caches = []
    for prefix_index in range(NPFX):
        caches.append(broadcast(prefix_cache, "req", prefix_owner[prefix_index]))
    stacked = jnp.concatenate(caches, axis=0)
    chosen = jnp.take(stacked, request_prefix, axis=0)
    attended = attend_local(queries, suffix_kv, chosen, suffix_len, requests, slot_len)
    partial_value = jnp.dot(attended, w_out, preferred_element_type=jnp.float32)
    summed_attn = lax.psum(partial_value.astype(jnp.bfloat16), "tp").astype(jnp.float32)
    hidden_state = residual.astype(jnp.float32) + summed_attn
    inverse = lax.rsqrt(jnp.mean(hidden_state * hidden_state, axis=1, keepdims=True) + 1e-05)
    scaled = hidden_state * norm_gain * inverse
    logits = jnp.dot(scaled, router, precision=lax.Precision.HIGHEST)
    normed_full = scaled.astype(jnp.bfloat16)
    hidden_share = lax.dynamic_slice_in_dim(hidden_state, share_start, share_width, 1)
    route_hit = (routes[:, :, None] == jnp.arange(EXPERTS, dtype=jnp.int32)).astype(jnp.float32)
    picked_logit = jnp.sum(route_hit * logits[:, None, :], axis=2)
    first_weight = jax.nn.sigmoid(picked_logit[:, 0] - picked_logit[:, 1])
    route_weight = jnp.stack([first_weight, 1.0 - first_weight], axis=1)
    live_rows = jnp.arange(routes.shape[0], dtype=jnp.int32) % slot_len < jnp.repeat(
        suffix_len, slot_len
    )
    placing, combining = routing_tables(routes, live_rows, route_weight)
    repeats = req_count // EXPERTS
    send_rows = jnp.dot(placing, normed_full, preferred_element_type=jnp.float32).astype(
        jnp.bfloat16
    )
    outgoing = jnp.tile(send_rows.reshape(EXPERTS, CAP, model_width), (repeats, 1, 1))
    returned = send_back(
        expert_apply(
            lax.all_to_all(outgoing, "req", split_axis=0, concat_axis=0, tiled=True),
            w_gate,
            w_up,
            w_down,
        )
    )
    summed = returned.astype(jnp.float32).reshape(repeats, EXPERTS, CAP, model_width).sum(axis=0)
    mixture_full = jnp.dot(
        combining, summed.reshape(EXPERTS * CAP, model_width), precision=lax.Precision.HIGHEST
    )
    mixture_share = lax.psum_scatter(
        mixture_full.astype(jnp.bfloat16), "tp", scatter_dimension=1, tiled=True
    ).astype(jnp.float32)
    layer_out = jnp.where(live_rows[:, None], hidden_share + mixture_share, 0.0)
    return layer_out.astype(jnp.bfloat16)


def solution(mesh):
    return jax.shard_map(
        per_device,
        mesh=mesh,
        in_specs=(
            P("req", "tp"),
            P("req", None, "tp"),
            P("req", None, None, "tp"),
            P(),
            P("req"),
            P("req"),
            P("req", None),
            P(),
            P(),
            P("req", None),
            P("req", None, "tp"),
            P("req", None, "tp"),
            P("req", "tp", None),
            P("tp", None),
        ),
        out_specs=P("req", "tp"),
        check_vma=False,
    )
```

profile of v0, /device:TPU:2, one launch (start us, length us, event | category | flops | bytes accessed | tf_op | source)
XLA Modules:
  0.0 477.0 jit_solution(7301594830305967729)
XLA Ops:
  6.5 1.5 fusion.63
  10.6 3.3 broadcast_select_fusion.3
  14.0 0.6 copy-done.12
  15.7 122.6 %all-reduce.6.cloned.1.call-done = (bf16[1,2048,2,128]{3,1,2,0:T(8,128)(2,1)}, bf16[1,2048,2,128]{3,1,2,0:T(8,128)(2,1)}, bf16[1,2048,2,128]{3,1,2,0:T(8,128)(2,1)}, bf16[1,2048,2,128]{3,1,2,0:T(8,128)(2,1)}) async-done(((bf16[1,2048,2,128]{3,1,2,0:T(8,128)(2,1)}, bf16[1,2048,2,128]{3,1,2,0:T(8,128)(2,1)}, bf16[1,2048,2,128]{3,1,2,0:T(8,128)(2,1)}, bf16[1,2048,2,128]{3,1,2,0:T(8,128)(2,1)}), ...) | async-done | bytes 4194320 | tf_op jit(solution)/shard_map/psum | solution.py:17
  138.4 3.7 pad_maximum_fusion
  142.1 4.4 gather_fusion
  146.5 1.9 bitcast_select_fusion
  148.3 0.5 fusion.64
  148.9 0.4 fusion.7
  149.3 0.6 fusion.22
  150.2 1.4 copy-done.1
  151.5 1.6 convolution_convert_fusion.2
  153.8 0.6 fusion.16
  154.5 73.0 %all-reduce.4.cloned.1.call-done = bf16[64,4096]{1,0:T(8,128)(2,1)} async-done(((bf16[64,4096]{1,0:T(8,128)(2,1)}), bf16[64,4096]{1,0:T(8,128)(2,1)}) %all-reduce.4.cloned.1.call-update) | async-done | bytes 524304 | tf_op jit(solution)/shard_map/psum | solution.py:134
  227.5 2.4 convert_add_fusion
  229.9 1.6 convolution_convert_fusion.1
  231.5 1.3 tile.10
  232.8 2.2 tile.11
  235.0 79.5 %all_to_all.10 = bf16[32,18,4096]{2,1,0:T(8,128)(2,1)} all-to-all(bf16[32,18,4096]{2,1,0:T(8,128)(2,1)S(1)} %bitcast.105), channel_id=1, replica_groups=mesh['req'=32,'tp'=8] {'req'}, dimensions={0} | all-to-all | bytes 9437184 | tf_op jit(solution)/shard_map/all_to_all | solution.py:156
  314.5 7.7 %reshape.205 = bf16[576,4096]{1,0:T(8,128)(2,1)} reshape(bf16[32,18,4096]{2,1,0:T(8,128)(2,1)} %all_to_all.10) | data formatting | bytes 9437184 | tf_op jit(solution)/shard_map/reshape | solution.py:89
  322.2 4.4 fusion.5
  326.6 10.2 %convolution_convert_fusion = bf16[576,4096]{1,0:T(8,128)(2,1)} fusion(bf16[1,256,4096]{2,1,0:T(8,128)(2,1)S(1)} %copy-done, bf16[576,4096]{1,0:T(8,128)(2,1)} %reshape.205, bf16[1,4096,256]{2,1,0:T(8,128)(2,1)} %param.25, f32[576,256]{1,0:T(8,128)S(1)} %fusion.5), kind=kOutput, calls=%fused_computation.2 | convolution fusion | flops 2419163136 | bytes 14221312 | tf_op jit(solution)/shard_map/dot_general | solution.py:93
  336.8 7.5 %reshape.206 = bf16[32,18,4096]{2,1,0:T(8,128)(2,1)} reshape(bf16[576,4096]{1,0:T(8,128)(2,1)} %convolution_convert_fusion) | data formatting | bytes 9437184 | tf_op jit(solution)/shard_map/reshape | solution.py:96
  344.4 6.1 %all-to-all-start.1 = ((bf16[32,18,4096]{2,1,0:T(8,128)(2,1)}), bf16[32,18,4096]{2,1,0:T(8,128)(2,1)}, u32[]{:S(2)}, u32[]{:S(2)}) async-start(bf16[32,18,4096]{2,1,0:T(8,128)(2,1)} %reshape.206), calls=%async_computation.1 | async-start | bytes 12582912 | tf_op jit(solution)/shard_map/all_to_all | solution.py:100
  350.5 0.3 reduce-scatter.2.cloned.1.call-start
  350.8 1.1 fusion.25
  352.4 0.7 fusion.40
  353.2 72.6 %all-to-all-done.1 = bf16[32,18,4096]{2,1,0:T(8,128)(2,1)} async-done(((bf16[32,18,4096]{2,1,0:T(8,128)(2,1)}), bf16[32,18,4096]{2,1,0:T(8,128)(2,1)}, u32[]{:S(2)}, u32[]{:S(2)}) %all-to-all-start.1) | async-done | bytes 4718624 | tf_op jit(solution)/shard_map/all_to_all | solution.py:100
  425.8 4.3 convert_reduce_fusion
  430.1 4.2 fusion
  434.3 34.5 %reduce-scatter.2.cloned.1.call-done = bf16[64,512]{1,0:T(8,128)(2,1)} async-done(((bf16[64,4096]{1,0:T(8,128)(2,1)}), bf16[64,512]{1,0:T(8,128)(2,1)}) %reduce-scatter.2.cloned.1.call-update) | async-done | bytes 65552 | tf_op jit(solution)/shard_map/reduce_scatter | solution.py:166
  468.8 1.7 select_convert_fusion
  (63 shorter events, 2.8 us)
Async XLA Ops:
  6.5 320.1 %copy-start = (bf16[1,256,4096]{2,1,0:T(8,128)(2,1)S(1)}, bf16[1,256,4096]{2,1,0:T(8,128)(2,1)}, u32[]{:S(2)}) copy-start(bf16[1,256,4096]{2,1,0:T(8,128)(2,1)} %param.26) | copy-start | bytes 6291460
  6.5 131.8 %all-reduce.6.cloned.1.call-start = ((), (), s32[]{:S(2)}) async-start(), calls=%async_computation.5 | async-start | bytes 8388608 | tf_op jit(solution)/shard_map/psum | solution.py:17
  13.9 0.7 copy-start.12
  13.9 1.1 copy-start.9
  13.9 1.3 copy-start.7
  13.9 1.3 copy-start.6
  13.9 1.4 copy-start.11
  14.0 213.5 %all-reduce.4.cloned.1.call-start = ((), (), s32[]{:S(2)}) async-start(), calls=%async_computation.3 | async-start | bytes 1048576 | tf_op jit(solution)/shard_map/psum | solution.py:134
  149.3 2.2 copy-start.1
  153.2 74.3 %copy-start.2 = (bf16[64,4096]{1,0:T(8,128)(2,1)S(1)}, bf16[64,4096]{1,0:T(8,128)(2,1)}, u32[]{:S(2)}) copy-start(bf16[64,4096]{1,0:T(8,128)(2,1)} %param.20) | copy-start | bytes 1572868
  153.2 76.7 %copy-start.8 = (f32[4096]{0:T(1024)S(1)}, f32[4096]{0:T(1024)}, u32[]{:S(2)}) copy-start(f32[4096]{0:T(1024)} %param.21) | copy-start | bytes 49156
  227.5 2.4 copy-start.4
  344.4 6.4 %copy-start.3 = (bf16[64,4096]{1,0:T(8,128)(2,1)S(1)}, bf16[64,4096]{1,0:T(8,128)(2,1)}, u32[]{:S(2)}) copy-start(bf16[64,4096]{1,0:T(8,128)(2,1)} %param.20) | copy-start | bytes 1572868
  344.4 6.4 %copy-start.5 = (bf16[64,4096]{1,0:T(8,128)(2,1)S(1)}, bf16[64,4096]{1,0:T(8,128)(2,1)}, u32[]{:S(2)}) copy-start(bf16[64,4096]{1,0:T(8,128)(2,1)} %all-reduce.4.cloned.1.call-done) | copy-start | bytes 1572868
  344.4 6.4 %copy-start.10 = (f32[4096,8]{0,1:T(8,128)S(1)}, f32[4096,8]{0,1:T(8,128)}, u32[]{:S(2)}) copy-start(f32[4096,8]{0,1:T(8,128)} %param.22) | copy-start | bytes 393220
  344.4 81.4 %all-to-all-start.1 = ((bf16[32,18,4096]{2,1,0:T(8,128)(2,1)}), bf16[32,18,4096]{2,1,0:T(8,128)(2,1)}, u32[]{:S(2)}, u32[]{:S(2)}) async-start(bf16[32,18,4096]{2,1,0:T(8,128)(2,1)} %reshape.206), calls=%async_computation.1 | async-start | bytes 12582912 | tf_op jit(solution)/shard_map/all_to_all | solution.py:100
  350.5 118.3 %reduce-scatter.2.cloned.1.call-start = ((), (), s32[]{:S(2)}) async-start(), calls=%async_computation.4 | async-start | bytes 589824 | tf_op jit(solution)/shard_map/reduce_scatter | solution.py:166
Sparse Core Ops, SparseCore 0:
  14.1 124.2 all-reduce.5
  153.3 74.1 all-reduce.3
  434.4 34.3 reduce-scatter.1
where the time goes:
time: 478 us; the launch traced here: 477 us
  waiting for transfers between devices  303 us (63%)
  blocking collectives  79.5 us (17%)
  local copies, waits for them, and re-layouts  27.9 us (6%)
  matrix products  25.9 us (5%)
  other arithmetic  18.6 us (4%)
  between operations  15.9 us (3%)
  starting transfers between devices  6.38 us (1%)
    psum x1, waiting for transfers between devices, broadcast(): return lax.psum(jnp.where(mine, x, jnp.zeros_like(x)), axis)  123 us
    all_to_all x1, blocking collectives, per_device(): lax.all_to_all(outgoing, 'req', split_axis=0, concat_axis=0, tiled=True)  79.5 us
    psum x1, waiting for transfers between devices, per_device(): lax.psum(partial_value.astype(jnp.bfloat16), 'tp').astype(jnp.float32)  73 us
    all_to_all x1, waiting for transfers between devices, send_back(): return lax.all_to_all(parts, 'req', split_axis=0, concat_axis=0, tiled=True)  72.6 us
    reduce_scatter x1, waiting for transfers between devices, per_device(): lax.psum_scatter(mixture_full.astype(jnp.bfloat16), 'tp', scatter_dimensi...  34.5 us
    dot_general x1, matrix products, expert_apply(): jnp.dot(hidden_units, w_down[0], preferred_element_type=jnp.float32)  10.2 us
  transfers between devices with their start and end apart: 4, of which 4 were waited for; matrix products, arithmetic and copies ran while one was open for 1% of the time, Pallas kernels for 0%

commit v1 on v0

--- a/solution.py
+++ b/solution.py
@@ -131,7 +131,9 @@
     chosen = jnp.take(stacked, request_prefix, axis=0)
     attended = attend_local(queries, suffix_kv, chosen, suffix_len, requests, slot_len)
     partial_value = jnp.dot(attended, w_out, preferred_element_type=jnp.float32)
-    summed_attn = lax.psum(partial_value.astype(jnp.bfloat16), "tp").astype(jnp.float32)
+    summed_attn = jnp.sum(lax.all_gather(partial_value.astype(jnp.bfloat16), "tp"), axis=0).astype(
+        jnp.float32
+    )
     hidden_state = residual.astype(jnp.float32) + summed_attn
     inverse = lax.rsqrt(jnp.mean(hidden_state * hidden_state, axis=1, keepdims=True) + 1e-05)
     scaled = hidden_state * norm_gain * inverse

time: 478 us -> 463 us (0.969)
  waiting for transfers between devices: 303 us -> 284 us
    psum x1 -> x0, waiting for transfers between devices: 73 us -> none  [per_device(): lax.psum(partial_value.astype(jnp.bfloat16), 'tp').astype(jnp.float32)]
    all_gather x0 -> x1, waiting for transfers between devices: none -> 53.3 us  [per_device(): lax.all_gather(partial_value.astype(jnp.bfloat16), 'tp')]
where the time goes in v1:
time: 463 us; the launch traced here: 462 us
  waiting for transfers between devices  284 us (61%)
  blocking collectives  79.5 us (17%)
  local copies, waits for them, and re-layouts  29.2 us (6%)
  matrix products  26.7 us (6%)
  other arithmetic  20.6 us (4%)
  between operations  15.9 us (3%)
  starting transfers between devices  6.38 us (1%)
    psum x1, waiting for transfers between devices, broadcast(): return lax.psum(jnp.where(mine, x, jnp.zeros_like(x)), axis)  123 us
    all_to_all x1, blocking collectives, per_device(): lax.all_to_all(outgoing, 'req', split_axis=0, concat_axis=0, tiled=True)  79.5 us
    all_to_all x1, waiting for transfers between devices, send_back(): return lax.all_to_all(parts, 'req', split_axis=0, concat_axis=0, tiled=True)  72.6 us
    all_gather x1, waiting for transfers between devices, per_device(): lax.all_gather(partial_value.astype(jnp.bfloat16), 'tp')  53.3 us
    reduce_scatter x1, waiting for transfers between devices, per_device(): lax.psum_scatter(mixture_full.astype(jnp.bfloat16), 'tp', scatter_dimensi...  34.7 us
    dot_general x1, matrix products, expert_apply(): jnp.dot(hidden_units, w_down[0], preferred_element_type=jnp.float32)  10.2 us
  transfers between devices with their start and end apart: 4, of which 4 were waited for; matrix products, arithmetic and copies ran while one was open for 1% of the time, Pallas kernels for 0%

profile of v1, /device:TPU:2, one launch (start us, length us, event | category | flops | bytes accessed | tf_op | source)
XLA Modules:
  0.0 462.1 jit_solution(1291881365897656098)
XLA Ops:
  6.5 1.5 fusion.63
  10.6 3.4 broadcast_select_fusion.3
  14.0 0.7 copy-done.4
  15.3 123.1 %all-reduce.3.cloned.1.call-done = (bf16[1,2048,2,128]{3,1,2,0:T(8,128)(2,1)}, bf16[1,2048,2,128]{3,1,2,0:T(8,128)(2,1)}, bf16[1,2048,2,128]{3,1,2,0:T(8,128)(2,1)}, bf16[1,2048,2,128]{3,1,2,0:T(8,128)(2,1)}) async-done(((bf16[1,2048,2,128]{3,1,2,0:T(8,128)(2,1)}, bf16[1,2048,2,128]{3,1,2,0:T(8,128)(2,1)}, bf16[1,2048,2,128]{3,1,2,0:T(8,128)(2,1)}, bf16[1,2048,2,128]{3,1,2,0:T(8,128)(2,1)}), ...) | async-done | bytes 4194320 | tf_op jit(solution)/shard_map/psum | solution.py:17
  138.4 3.7 pad_maximum_fusion
  142.1 4.3 gather_fusion
  146.4 1.9 bitcast_select_fusion
  148.3 0.5 fusion.64
  148.9 0.4 fusion.7
  149.3 0.6 fusion.22
  150.2 1.4 copy-done.1
  151.5 1.6 convolution_convert_fusion.2
  154.4 0.6 fusion.16
  155.1 53.3 %all-gather.3.cloned.1.call-done = bf16[512,4096]{1,0:T(8,128)(2,1)} async-done(((bf16[64,4096]{1,0:T(8,128)(2,1)}), bf16[512,4096]{1,0:T(8,128)(2,1)}) %all-gather.3.cloned.1.call-update) | async-done | bytes 4194320 | tf_op jit(solution)/shard_map/all_gather | solution.py:134
  208.5 3.0 reduce_sum.68
  211.5 1.3 convert_add_fusion
  212.8 1.5 convolution_convert_fusion.1
  214.4 2.4 tile.10
  216.8 2.2 tile.11
  218.9 79.5 %all_to_all.10 = bf16[32,18,4096]{2,1,0:T(8,128)(2,1)} all-to-all(bf16[32,18,4096]{2,1,0:T(8,128)(2,1)S(1)} %bitcast.106), channel_id=1, replica_groups=mesh['req'=32,'tp'=8] {'req'}, dimensions={0} | all-to-all | bytes 9437184 | tf_op jit(solution)/shard_map/all_to_all | solution.py:158
  298.4 7.8 %reshape.205 = bf16[576,4096]{1,0:T(8,128)(2,1)} reshape(bf16[32,18,4096]{2,1,0:T(8,128)(2,1)} %all_to_all.10) | data formatting | bytes 9437184 | tf_op jit(solution)/shard_map/reshape | solution.py:89
  306.2 5.2 %fusion.5 = f32[576,256]{1,0:T(8,128)} fusion(bf16[576,4096]{1,0:T(8,128)(2,1)} %reshape.205, bf16[1,4096,256]{2,1,0:T(8,128)(2,1)} %param.24), kind=kOutput, calls=%fused_computation.13 | convolution fusion | flops 1207959552 | bytes 7405568 | tf_op jit(solution)/shard_map/dot_general | solution.py:90
  311.4 10.2 %convolution_convert_fusion = bf16[576,4096]{1,0:T(8,128)(2,1)} fusion(bf16[1,256,4096]{2,1,0:T(8,128)(2,1)S(1)} %copy-done, bf16[576,4096]{1,0:T(8,128)(2,1)} %reshape.205, bf16[1,4096,256]{2,1,0:T(8,128)(2,1)} %param.25, f32[576,256]{1,0:T(8,128)} %fusion.5), kind=kOutput, calls=%fused_computation.2 | convolution fusion | flops 2419163136 | bytes 14221312 | tf_op jit(solution)/shard_map/dot_general | solution.py:93
  321.7 7.6 %reshape.206 = bf16[32,18,4096]{2,1,0:T(8,128)(2,1)} reshape(bf16[576,4096]{1,0:T(8,128)(2,1)} %convolution_convert_fusion) | data formatting | bytes 9437184 | tf_op jit(solution)/shard_map/reshape | solution.py:96
  329.3 6.1 %all-to-all-start.1 = ((bf16[32,18,4096]{2,1,0:T(8,128)(2,1)}), bf16[32,18,4096]{2,1,0:T(8,128)(2,1)}, u32[]{:S(2)}, u32[]{:S(2)}) async-start(bf16[32,18,4096]{2,1,0:T(8,128)(2,1)} %reshape.206), calls=%async_computation.1 | async-start | bytes 12582912 | tf_op jit(solution)/shard_map/all_to_all | solution.py:100
  335.7 1.1 fusion.25
  337.3 0.7 fusion.40
  338.1 72.6 %all-to-all-done.1 = bf16[32,18,4096]{2,1,0:T(8,128)(2,1)} async-done(((bf16[32,18,4096]{2,1,0:T(8,128)(2,1)}), bf16[32,18,4096]{2,1,0:T(8,128)(2,1)}, u32[]{:S(2)}, u32[]{:S(2)}) %all-to-all-start.1) | async-done | bytes 4718624 | tf_op jit(solution)/shard_map/all_to_all | solution.py:100
  410.7 4.3 convert_reduce_fusion
  415.0 4.2 fusion
  419.2 34.7 %reduce-scatter.2.cloned.1.call-done = bf16[64,512]{1,0:T(8,128)(2,1)} async-done(((bf16[64,4096]{1,0:T(8,128)(2,1)}), bf16[64,512]{1,0:T(8,128)(2,1)}) %reduce-scatter.2.cloned.1.call-update) | async-done | bytes 65552 | tf_op jit(solution)/shard_map/reduce_scatter | solution.py:168
  453.9 1.7 select_convert_fusion
  (58 shorter events, 3.2 us)
Async XLA Ops:
  6.5 304.9 %copy-start = (bf16[1,256,4096]{2,1,0:T(8,128)(2,1)S(1)}, bf16[1,256,4096]{2,1,0:T(8,128)(2,1)}, u32[]{:S(2)}) copy-start(bf16[1,256,4096]{2,1,0:T(8,128)(2,1)} %param.26) | copy-start | bytes 6291460
  6.5 131.8 %all-reduce.3.cloned.1.call-start = ((), (), s32[]{:S(2)}) async-start(), calls=%async_computation.5 | async-start | bytes 8388608 | tf_op jit(solution)/shard_map/psum | solution.py:17
  14.0 0.8 copy-start.4
  14.0 0.9 copy-start.3
  14.0 0.9 copy-start.8
  14.0 0.9 copy-start.9
  14.0 194.5 %all-gather.3.cloned.1.call-start = ((), (), s32[]{:S(2)}) async-start(), calls=%async_computation.4 | async-start | bytes 4718592 | tf_op jit(solution)/shard_map/all_gather | solution.py:134
  149.3 2.2 copy-start.1
  151.5 2.1 copy-start.6
  208.5 3.0 copy-start.2
  211.5 1.3 copy-start.5
  329.3 6.4 %copy-start.7 = (f32[4096,8]{0,1:T(8,128)S(1)}, f32[4096,8]{0,1:T(8,128)}, u32[]{:S(2)}) copy-start(f32[4096,8]{0,1:T(8,128)} %param.22) | copy-start | bytes 393220
  329.3 81.4 %all-to-all-start.1 = ((bf16[32,18,4096]{2,1,0:T(8,128)(2,1)}), bf16[32,18,4096]{2,1,0:T(8,128)(2,1)}, u32[]{:S(2)}, u32[]{:S(2)}) async-start(bf16[32,18,4096]{2,1,0:T(8,128)(2,1)} %reshape.206), calls=%async_computation.1 | async-start | bytes 12582912 | tf_op jit(solution)/shard_map/all_to_all | solution.py:100
  335.4 118.5 %reduce-scatter.2.cloned.1.call-start = ((), (), s32[]{:S(2)}) async-start(), calls=%async_computation.3 | async-start | bytes 589824 | tf_op jit(solution)/shard_map/reduce_scatter | solution.py:168
Sparse Core Ops, SparseCore 0:
  14.1 124.2 all-reduce.2
  153.3 55.1 all-gather.2
  419.3 34.5 reduce-scatter.1
